TPU v7x, 256 devices: a whole 4x4x8 slice. The times are simulated.
256 devices in a mesh: ctx: 64 (over y_lo, z, x), fsdp: 4 (over y_hi, core).
Axes of the slice: x: 4, y: 4 (y_hi: 2, y_lo: 2; y = y_hi * 2 + y_lo), z: 8, core: 2. Of those that a mesh axis runs over, the one named last changes fastest.
Arguments:
- query: bfloat16 [16384, 2048], P('ctx', 'fsdp'), may hold values from -11 to 11
- key: bfloat16 [16384, 2048], P('ctx', 'fsdp'), may hold values from -11 to 11
- value: bfloat16 [16384, 2048], P('ctx', 'fsdp'), may hold values from -6 to 6
- doc_ids: int32 [16384], P('ctx'), may hold values from 0 to 19, never falling along the last dimension, each value on 1 to 2048 neighbouring positions
- out_weight: bfloat16 [2048, 4096], P(('fsdp', 'ctx')), may hold values from -0.125 to 0.125
- grad_out: bfloat16 [16384, 4096], P('ctx', 'fsdp'), may hold values from -6 to 6
Outputs:
- grad_query: bfloat16 [16384, 2048], P('ctx', 'fsdp')
- grad_key: bfloat16 [16384, 2048], P('ctx', 'fsdp')
- grad_value: bfloat16 [16384, 2048], P('ctx', 'fsdp')
- grad_out_weight: float32 [2048, 4096], P(('fsdp', 'ctx'))
Inputs may be any that keep to these rules, and one draw needn't show every extreme that they name: `doc_ids`: document ids never fall along the sequence; every document has 1 to 2048 tokens and one has exactly 2048.
All inputs are finite; a program needn't handle non-finite values.
Results may differ from a plain program's by a relative error of at most 0.034.
Values may be sent and summed in bfloat16 or wider, within the bound.
No kernel may reach another device: no remote copies, remote signals or barrier semaphores. Data moves between devices by JAX's collectives and lax.ppermute only.
A program may use at most 128 MiB of HBM per device.

v0:
```python
import math
import jax
import jax.numpy as jnp
from jax import lax
from jax.sharding import PartitionSpec as P

DH = 128
NEGATIVE = -1e30


def shifted(array, axis, by):
    devices = lax.axis_size(axis)
    pairs = [(i, i + by) for i in range(devices) if 0 <= i + by < devices]
    return lax.ppermute(array, axis, pairs)


def as_sent(array):

    def short(part):
        return part.astype(jnp.bfloat16) if part.dtype == jnp.float32 else part

    return jax.tree.map(short, array)


def passed_along(block, axis, distance):
    devices = range(lax.axis_size(axis))
    route = [((i - distance) % len(devices), i) for i in devices]
    return lax.ppermute(block, axis, route)


def shards(query, key, value, doc_ids, out_weight, grad_out):
    tok_rows = query.shape[0]
    feature_width = query.shape[1]
    head_count = feature_width // DH
    cycle_size = lax.axis_size("ctx")
    cycle_reach = max(cycle_size // 8, 2)
    cycle_index = lax.axis_index("ctx")
    score_scale = 1.0 / math.sqrt(DH)
    local_pos = jnp.arange(tok_rows, dtype=jnp.int32)
    own_pos = cycle_index * tok_rows + local_pos
    own_docs = doc_ids + 1
    query_heads = query.reshape(tok_rows, head_count, DH)
    key_heads = key.reshape(tok_rows, head_count, DH)
    value_heads = value.reshape(tok_rows, head_count, DH)

    def scores_of(query_block, key_block):
        return (
            jnp.einsum("tnd,snd->nts", query_block, key_block, preferred_element_type=jnp.float32)
            * score_scale
        )

    state = (
        jnp.full((head_count, tok_rows), NEGATIVE, jnp.float32),
        jnp.zeros((head_count, tok_rows), jnp.float32),
        jnp.zeros((head_count, tok_rows, DH), jnp.float32),
    )
    key_block, value_block = (key_heads, value_heads)
    key_docs = own_docs
    stored_blocks = []
    for cycle_step in range(cycle_reach + 1):
        if cycle_step > 0:
            key_block, value_block = shifted((key_block, value_block), "ctx", 1)
            key_docs = shifted(key_docs, "ctx", 1)
        key_pos = own_pos - cycle_step * tok_rows
        pair_mask = (own_docs[:, None] == key_docs[None, :]) & (
            key_pos[None, :] <= own_pos[:, None]
        )
        forward_row_max, forward_row_sum, forward_output_sum = state
        forward_scores = jnp.where(pair_mask[None], scores_of(query_heads, key_block), NEGATIVE)
        new_max = jnp.maximum(forward_row_max, jnp.max(forward_scores, axis=-1))
        decay_factor = jnp.exp(forward_row_max - new_max)
        forward_weights = jnp.where(
            pair_mask[None], jnp.exp(forward_scores - new_max[..., None]), 0.0
        )
        new_sum = forward_row_sum * decay_factor + jnp.sum(forward_weights, axis=-1)
        weights_low = forward_weights.astype(jnp.bfloat16)
        new_output = forward_output_sum * decay_factor[..., None] + jnp.einsum(
            "nts,snd->ntd", weights_low, value_block, preferred_element_type=jnp.float32
        )
        state = (new_max, new_sum, new_output)
        stored_blocks.append((key_block, value_block, pair_mask))
    row_max, row_sum, output_sum = state
    log_total = row_max + jnp.log(row_sum)
    attn_heads = (output_sum / row_sum[..., None]).astype(jnp.bfloat16).transpose(1, 0, 2)
    attention = attn_heads.reshape(tok_rows, feature_width)
    grad_full = lax.all_gather(grad_out, "fsdp", axis=1, tiled=True)
    grad_attn = lax.dot_general(
        grad_full,
        lax.all_gather(out_weight, "ctx", axis=0, tiled=True),
        (((1,), (1,)), ((), ())),
        preferred_element_type=jnp.float32,
    ).astype(jnp.bfloat16)
    grad_weight = lax.psum_scatter(
        lax.dot_general(
            attention, grad_full, (((0,), (0,)), ((), ())), preferred_element_type=jnp.float32
        ),
        "ctx",
        scatter_dimension=0,
        tiled=True,
    )
    grad_heads = grad_attn.reshape(tok_rows, head_count, DH)
    delta_sum = jnp.einsum(
        "tnd,tnd->nt", grad_heads, attn_heads, preferred_element_type=jnp.float32
    )
    grad_query = jnp.zeros((tok_rows, head_count, DH), jnp.float32)
    carried = None
    for cycle_step in range(cycle_reach + 1):
        key_block, value_block, pair_mask = stored_blocks[cycle_step]
        if cycle_step > 0:
            carried = jax.tree.map(
                lambda part, own: part.astype(own.dtype),
                passed_along(as_sent(carried), "ctx", 1),
                carried,
            )
        scores = scores_of(query_heads, key_block)
        weights = jnp.where(pair_mask[None], jnp.exp(scores - log_total[..., None]), 0.0)
        rounded = weights.astype(jnp.bfloat16)
        value_part = jnp.einsum(
            "nts,tnd->snd", rounded, grad_heads, preferred_element_type=jnp.float32
        )
        grad_weights = jnp.einsum(
            "tnd,snd->nts", grad_heads, value_block, preferred_element_type=jnp.float32
        )
        grad_scores = (weights * (grad_weights - delta_sum[..., None])).astype(jnp.bfloat16)
        query_part = (
            jnp.einsum("nts,snd->tnd", grad_scores, key_block, preferred_element_type=jnp.float32)
            * score_scale
        )
        key_part = (
            jnp.einsum("nts,tnd->snd", grad_scores, query_heads, preferred_element_type=jnp.float32)
            * score_scale
        )
        query_part, key_part, value_part = (query_part, key_part, value_part)
        grad_query = grad_query + query_part
        if cycle_step == 0:
            carried = (key_part, value_part)
        else:
            carried = (carried[0] + key_part, carried[1] + value_part)
    grad_key, grad_value = jax.tree.map(
        lambda part, own: part.astype(own.dtype),
        passed_along(as_sent(carried), "ctx", -cycle_reach),
        carried,
    )
    return (
        grad_query.reshape(tok_rows, feature_width).astype(jnp.bfloat16),
        grad_key.reshape(tok_rows, feature_width).astype(jnp.bfloat16),
        grad_value.reshape(tok_rows, feature_width).astype(jnp.bfloat16),
        grad_weight,
    )


def solution(mesh):
    return jax.shard_map(
        shards,
        mesh=mesh,
        in_specs=(
            P("ctx", "fsdp"),
            P("ctx", "fsdp"),
            P("ctx", "fsdp"),
            P("ctx"),
            P(("fsdp", "ctx"), None),
            P("ctx", "fsdp"),
        ),
        out_specs=(P("ctx", "fsdp"), P("ctx", "fsdp"), P("ctx", "fsdp"), P(("fsdp", "ctx"), None)),
        check_vma=False,
    )
```

profile of v0, /device:TPU:8, one launch (start us, length us, event | category | flops | bytes accessed | tf_op | source)
XLA Modules:
  0.0 712.0 jit_solution(2859584681869793939)
XLA Ops:
  12.8 8.0 %collective-permute-done = s32[256]{0:T(256)S(1)} collective-permute-done((s32[256]{0:T(256)S(1)}, s32[256]{0:T(256)S(1)}, u32[]{:S(2)}, u32[]{:S(2)}) %collective-permute-start) | collective-permute-done | bytes 1056 | tf_op jit(solution)/shard_map/ppermute | solution.py:14
  22.7 7.8 %collective-permute-done.2 = s32[256]{0:T(256)S(1)} collective-permute-done((s32[256]{0:T(256)S(1)}, s32[256]{0:T(256)S(1)}, u32[]{:S(2)}, u32[]{:S(2)}) %collective-permute-start.2) | collective-permute-done | bytes 1056 | tf_op jit(solution)/shard_map/ppermute | solution.py:14
  42.1 9.6 %collective-permute-done.6 = s32[256]{0:T(256)S(1)} collective-permute-done((s32[256]{0:T(256)S(1)}, s32[256]{0:T(256)S(1)}, u32[]{:S(2)}, u32[]{:S(2)}) %collective-permute-start.6) | collective-permute-done | bytes 1056 | tf_op jit(solution)/shard_map/ppermute | solution.py:14
  53.6 7.7 %collective-permute-done.8 = s32[256]{0:T(256)S(1)} collective-permute-done((s32[256]{0:T(256)S(1)}, s32[256]{0:T(256)S(1)}, u32[]{:S(2)}, u32[]{:S(2)}) %collective-permute-start.8) | collective-permute-done | bytes 1056 | tf_op jit(solution)/shard_map/ppermute | solution.py:14
  63.3 7.8 %collective-permute-done.10 = s32[256]{0:T(256)S(1)} collective-permute-done((s32[256]{0:T(256)S(1)}, s32[256]{0:T(256)S(1)}, u32[]{:S(2)}, u32[]{:S(2)}) %collective-permute-start.10) | collective-permute-done | bytes 1056 | tf_op jit(solution)/shard_map/ppermute | solution.py:14
  73.0 7.7 %collective-permute-done.12 = s32[256]{0:T(256)S(1)} collective-permute-done((s32[256]{0:T(256)S(1)}, s32[256]{0:T(256)S(1)}, u32[]{:S(2)}, u32[]{:S(2)}) %collective-permute-start.12) | collective-permute-done | bytes 1056 | tf_op jit(solution)/shard_map/ppermute | solution.py:14
  82.6 7.7 %collective-permute-done.14 = s32[256]{0:T(256)S(1)} collective-permute-done((s32[256]{0:T(256)S(1)}, s32[256]{0:T(256)S(1)}, u32[]{:S(2)}, u32[]{:S(2)}) %collective-permute-start.14) | collective-permute-done | bytes 1056 | tf_op jit(solution)/shard_map/ppermute | solution.py:14
  95.9 9.4 %collective-permute-done.3 = bf16[256,4,128]{2,0,1:T(8,128)(2,1)S(1)} collective-permute-done((bf16[256,4,128]{2,0,1:T(8,128)(2,1)S(1)}, bf16[256,4,128]{2,0,1:T(8,128)(2,1)S(1)}, u32[]{:S(2)}, u32[]{:S(2)}) %collective-permute-start.3) | collective-permute-done | bytes 262176 | tf_op jit(solution)/shard_map/ppermute | solution.py:14
  120.5 7.6 %collective-permute-done.18 = bf16[256,4,128]{0,2,1:T(8,128)(2,1)S(1)} collective-permute-done((bf16[256,4,128]{0,2,1:T(8,128)(2,1)S(1)}, bf16[256,4,128]{0,2,1:T(8,128)(2,1)S(1)}, u32[]{:S(2)}, u32[]{:S(2)}) %collective-permute-start.18) | collective-permute-done | bytes 262176 | tf_op jit(solution)/shard_map/ppermute | solution.py:14
  135.9 6.3 collective-permute-done.19
  157.4 7.1 %collective-permute-done.11 = bf16[256,4,128]{2,0,1:T(8,128)(2,1)S(1)} collective-permute-done((bf16[256,4,128]{2,0,1:T(8,128)(2,1)S(1)}, bf16[256,4,128]{2,0,1:T(8,128)(2,1)S(1)}, u32[]{:S(2)}, u32[]{:S(2)}) %collective-permute-start.11) | collective-permute-done | bytes 262176 | tf_op jit(solution)/shard_map/ppermute | solution.py:14
  172.7 6.6 collective-permute-done.13
  201.0 145.4 %all-gather.5.cloned.1.call-done = bf16[512,4096]{1,0:T(8,128)(2,1)} async-done(((bf16[8,4096]{1,0:T(8,128)(2,1)}), bf16[512,4096]{1,0:T(8,128)(2,1)}) %all-gather.5.cloned.1.call-update) | async-done | bytes 4194320 | tf_op jit(solution)/shard_map/all_gather | solution.py:89
  382.2 6.9 collective-permute-done.33
  389.9 8.2 %collective-permute-done.25 = bf16[256,4,128]{0,2,1:T(8,128)(2,1)S(1)} collective-permute-done((bf16[256,4,128]{0,2,1:T(8,128)(2,1)S(1)}, bf16[256,4,128]{0,2,1:T(8,128)(2,1)S(1)}, u32[]{:S(2)}, u32[]{:S(2)}) %collective-permute-start.25) | collective-permute-done | bytes 262176 | tf_op jit(solution)/shard_map/ppermute | solution.py:28
  398.2 8.1 %collective-permute-done.34 = bf16[256,4,128]{0,2,1:T(8,128)(2,1)S(1)} collective-permute-done((bf16[256,4,128]{0,2,1:T(8,128)(2,1)S(1)}, bf16[256,4,128]{0,2,1:T(8,128)(2,1)S(1)}, u32[]{:S(2)}, u32[]{:S(2)}) %collective-permute-start.34) | collective-permute-done | bytes 262176 | tf_op jit(solution)/shard_map/ppermute | solution.py:28
  407.1 6.8 collective-permute-done.26
  414.0 7.5 %collective-permute-done.35 = bf16[256,4,128]{0,2,1:T(8,128)(2,1)S(1)} collective-permute-done((bf16[256,4,128]{0,2,1:T(8,128)(2,1)S(1)}, bf16[256,4,128]{0,2,1:T(8,128)(2,1)S(1)}, u32[]{:S(2)}, u32[]{:S(2)}) %collective-permute-start.35) | collective-permute-done | bytes 262176 | tf_op jit(solution)/shard_map/ppermute | solution.py:28
  422.3 6.5 collective-permute-done.27
  433.8 7.6 %collective-permute-done.28 = bf16[256,4,128]{0,2,1:T(8,128)(2,1)S(1)} collective-permute-done((bf16[256,4,128]{0,2,1:T(8,128)(2,1)S(1)}, bf16[256,4,128]{0,2,1:T(8,128)(2,1)S(1)}, u32[]{:S(2)}, u32[]{:S(2)}) %collective-permute-start.28) | collective-permute-done | bytes 262176 | tf_op jit(solution)/shard_map/ppermute | solution.py:28
  445.7 7.2 %collective-permute-done.29 = bf16[256,4,128]{0,2,1:T(8,128)(2,1)S(1)} collective-permute-done((bf16[256,4,128]{0,2,1:T(8,128)(2,1)S(1)}, bf16[256,4,128]{0,2,1:T(8,128)(2,1)S(1)}, u32[]{:S(2)}, u32[]{:S(2)}) %collective-permute-start.29) | collective-permute-done | bytes 262176 | tf_op jit(solution)/shard_map/ppermute | solution.py:28
  457.8 6.4 collective-permute-done.30
  484.6 6.3 collective-permute-done.41
  491.8 213.5 %reduce-scatter.2.cloned.1.call-done = f32[8,4096]{1,0:T(8,128)} async-done(((f32[512,4096]{1,0:T(8,128)}), f32[8,4096]{1,0:T(8,128)}) %reduce-scatter.2.cloned.1.call-update) | async-done | bytes 131088 | tf_op jit(solution)/shard_map/reduce_scatter | solution.py:93
  (352 shorter events, 172.4 us)
Async XLA Ops:
  7.2 193.8 %all-gather.3.cloned.1.call-start = ((), (), s32[]{:S(2)}) async-start(), calls=%async_computation.1 | async-start | bytes 2621440 | tf_op jit(solution)/shard_map/all_gather | solution.py:86
  7.9 338.5 %all-gather.5.cloned.1.call-start = ((), (), s32[]{:S(2)}) async-start(), calls=%async_computation.2 | async-start | bytes 4259840 | tf_op jit(solution)/shard_map/all_gather | solution.py:89
  8.7 696.6 %reduce-scatter.2.cloned.1.call-start = ((), (), s32[]{:S(2)}) async-start(), calls=%async_computation.3 | async-start | bytes 8519680 | tf_op jit(solution)/shard_map/reduce_scatter | solution.py:93
  33.6 58.0 %collective-permute-start.1 = (bf16[256,4,128]{2,0,1:T(8,128)(2,1)S(1)}, bf16[256,4,128]{2,0,1:T(8,128)(2,1)S(1)}, u32[]{:S(2)}, u32[]{:S(2)}) collective-permute-start(bf16[256,4,128]{2,0,1:T(8,128)(2,1)S(1)} %copy.116), channel_id=1, source_target_pairs={{0,4},{4,8},{8,12},{12,16},{16,20},{20,24},{24,28},{28,32},{32,36}... | collective-permute-start | bytes 786440 | tf_op jit(solution)/shard_map/ppermute | solution.py:14
  36.7 56.9 %collective-permute-start.16 = (bf16[256,4,128]{0,2,1:T(8,128)(2,1)S(1)}, bf16[256,4,128]{0,2,1:T(8,128)(2,1)S(1)}, u32[]{:S(2)}, u32[]{:S(2)}) collective-permute-start(bf16[256,4,128]{0,2,1:T(8,128)(2,1)S(1)} %bitcast.466), channel_id=1, source_target_pairs={{0,4},{4,8},{8,12},{12,16},{16,20},{20,24},{24,28},{28,32},{32,36}... | collective-permute-start | bytes 786440 | tf_op jit(solution)/shard_map/ppermute | solution.py:14
  91.7 13.6 %collective-permute-start.3 = (bf16[256,4,128]{2,0,1:T(8,128)(2,1)S(1)}, bf16[256,4,128]{2,0,1:T(8,128)(2,1)S(1)}, u32[]{:S(2)}, u32[]{:S(2)}) collective-permute-start(bf16[256,4,128]{2,0,1:T(8,128)(2,1)S(1)} %collective-permute-done.1), channel_id=1, source_target_pairs={{0,4},{4,8},{8,12},{12,16},{16,20},{20,24},{24,28},{28,32},{32,36}... | collective-permute-start | bytes 786440 | tf_op jit(solution)/shard_map/ppermute | solution.py:14
  93.6 17.8 %collective-permute-start.17 = (bf16[256,4,128]{0,2,1:T(8,128)(2,1)S(1)}, bf16[256,4,128]{0,2,1:T(8,128)(2,1)S(1)}, u32[]{:S(2)}, u32[]{:S(2)}) collective-permute-start(bf16[256,4,128]{0,2,1:T(8,128)(2,1)S(1)} %collective-permute-done.16), channel_id=1, source_target_pairs={{0,4},{4,8},{8,12},{12,16},{16,20},{20,24},{24,28},{28,32},{32,36}... | collective-permute-start | bytes 786440 | tf_op jit(solution)/shard_map/ppermute | solution.py:14
  105.3 13.3 %collective-permute-start.5 = (bf16[256,4,128]{2,0,1:T(8,128)(2,1)S(1)}, bf16[256,4,128]{2,0,1:T(8,128)(2,1)S(1)}, u32[]{:S(2)}, u32[]{:S(2)}) collective-permute-start(bf16[256,4,128]{2,0,1:T(8,128)(2,1)S(1)} %collective-permute-done.3), channel_id=1, source_target_pairs={{0,4},{4,8},{8,12},{12,16},{16,20},{20,24},{24,28},{28,32},{32,36}... | collective-permute-start | bytes 786440 | tf_op jit(solution)/shard_map/ppermute | solution.py:14
  111.4 16.6 %collective-permute-start.18 = (bf16[256,4,128]{0,2,1:T(8,128)(2,1)S(1)}, bf16[256,4,128]{0,2,1:T(8,128)(2,1)S(1)}, u32[]{:S(2)}, u32[]{:S(2)}) collective-permute-start(bf16[256,4,128]{0,2,1:T(8,128)(2,1)S(1)} %collective-permute-done.17), channel_id=1, source_target_pairs={{0,4},{4,8},{8,12},{12,16},{16,20},{20,24},{24,28},{28,32},{32,36}... | collective-permute-start | bytes 786440 | tf_op jit(solution)/shard_map/ppermute | solution.py:14
  118.6 15.4 %collective-permute-start.7 = (bf16[256,4,128]{2,0,1:T(8,128)(2,1)S(1)}, bf16[256,4,128]{2,0,1:T(8,128)(2,1)S(1)}, u32[]{:S(2)}, u32[]{:S(2)}) collective-permute-start(bf16[256,4,128]{2,0,1:T(8,128)(2,1)S(1)} %collective-permute-done.5), channel_id=1, source_target_pairs={{0,4},{4,8},{8,12},{12,16},{16,20},{20,24},{24,28},{28,32},{32,36}... | collective-permute-start | bytes 786440 | tf_op jit(solution)/shard_map/ppermute | solution.py:14
  128.0 14.1 %collective-permute-start.19 = (bf16[256,4,128]{0,2,1:T(8,128)(2,1)S(1)}, bf16[256,4,128]{0,2,1:T(8,128)(2,1)S(1)}, u32[]{:S(2)}, u32[]{:S(2)}) collective-permute-start(bf16[256,4,128]{0,2,1:T(8,128)(2,1)S(1)} %collective-permute-done.18), channel_id=1, source_target_pairs={{0,4},{4,8},{8,12},{12,16},{16,20},{20,24},{24,28},{28,32},{32,36}... | collective-permute-start | bytes 786440 | tf_op jit(solution)/shard_map/ppermute | solution.py:14
  134.0 15.4 %collective-permute-start.9 = (bf16[256,4,128]{2,0,1:T(8,128)(2,1)S(1)}, bf16[256,4,128]{2,0,1:T(8,128)(2,1)S(1)}, u32[]{:S(2)}, u32[]{:S(2)}) collective-permute-start(bf16[256,4,128]{2,0,1:T(8,128)(2,1)S(1)} %collective-permute-done.7), channel_id=1, source_target_pairs={{0,4},{4,8},{8,12},{12,16},{16,20},{20,24},{24,28},{28,32},{32,36}... | collective-permute-start | bytes 786440 | tf_op jit(solution)/shard_map/ppermute | solution.py:14
  149.3 15.2 %collective-permute-start.11 = (bf16[256,4,128]{2,0,1:T(8,128)(2,1)S(1)}, bf16[256,4,128]{2,0,1:T(8,128)(2,1)S(1)}, u32[]{:S(2)}, u32[]{:S(2)}) collective-permute-start(bf16[256,4,128]{2,0,1:T(8,128)(2,1)S(1)} %collective-permute-done.9), channel_id=1, source_target_pairs={{0,4},{4,8},{8,12},{12,16},{16,20},{20,24},{24,28},{28,32},{32,36}... | collective-permute-start | bytes 786440 | tf_op jit(solution)/shard_map/ppermute | solution.py:14
  155.2 15.3 %collective-permute-start.21 = (bf16[256,4,128]{0,2,1:T(8,128)(2,1)S(1)}, bf16[256,4,128]{0,2,1:T(8,128)(2,1)S(1)}, u32[]{:S(2)}, u32[]{:S(2)}) collective-permute-start(bf16[256,4,128]{0,2,1:T(8,128)(2,1)S(1)} %collective-permute-done.20), channel_id=1, source_target_pairs={{0,4},{4,8},{8,12},{12,16},{16,20},{20,24},{24,28},{28,32},{32,36}... | collective-permute-start | bytes 786440 | tf_op jit(solution)/shard_map/ppermute | solution.py:14
  164.6 14.8 %collective-permute-start.13 = (bf16[256,4,128]{2,0,1:T(8,128)(2,1)S(1)}, bf16[256,4,128]{2,0,1:T(8,128)(2,1)S(1)}, u32[]{:S(2)}, u32[]{:S(2)}) collective-permute-start(bf16[256,4,128]{2,0,1:T(8,128)(2,1)S(1)} %collective-permute-done.11), channel_id=1, source_target_pairs={{0,4},{4,8},{8,12},{12,16},{16,20},{20,24},{24,28},{28,32},{32,36}... | collective-permute-start | bytes 786440 | tf_op jit(solution)/shard_map/ppermute | solution.py:14
  170.5 16.4 %collective-permute-start.22 = (bf16[256,4,128]{0,2,1:T(8,128)(2,1)S(1)}, bf16[256,4,128]{0,2,1:T(8,128)(2,1)}, u32[]{:S(2)}, u32[]{:S(2)}) collective-permute-start(bf16[256,4,128]{0,2,1:T(8,128)(2,1)S(1)} %collective-permute-done.21), channel_id=1, source_target_pairs={{0,4},{4,8},{8,12},{12,16},{16,20},{20,24},{24,28},{28,32},{32,36}... | collective-permute-start | bytes 786440 | tf_op jit(solution)/shard_map/ppermute | solution.py:14
  186.9 169.9 %collective-permute-start.23 = (bf16[256,4,128]{0,2,1:T(8,128)(2,1)}, bf16[256,4,128]{0,2,1:T(8,128)(2,1)}, u32[]{:S(2)}, u32[]{:S(2)}) collective-permute-start(bf16[256,4,128]{0,2,1:T(8,128)(2,1)} %collective-permute-done.22), channel_id=1, source_target_pairs={{0,4},{4,8},{8,12},{12,16},{16,20},{20,24},{24,28},{28,32},{32,36}... | collective-permute-start | bytes 786440 | tf_op jit(solution)/shard_map/ppermute | solution.py:14
  366.9 14.9 %collective-permute-start.24 = (bf16[256,4,128]{0,2,1:T(8,128)(2,1)S(1)}, bf16[256,4,128]{0,2,1:T(8,128)(2,1)S(1)}, u32[]{:S(2)}, u32[]{:S(2)}) collective-permute-start(bf16[256,4,128]{0,2,1:T(8,128)(2,1)S(1)} %fusion.49), channel_id=1, source_target_pairs={{252,0},{0,4},{4,8},{8,12},{12,16},{16,20},{20,24},{24,28},{28,32}... | collective-permute-start | bytes 786440 | tf_op jit(solution)/shard_map/ppermute | solution.py:28
  367.6 21.5 %collective-permute-start.33 = (bf16[256,4,128]{0,2,1:T(8,128)(2,1)S(1)}, bf16[256,4,128]{0,2,1:T(8,128)(2,1)S(1)}, u32[]{:S(2)}, u32[]{:S(2)}) collective-permute-start(bf16[256,4,128]{0,2,1:T(8,128)(2,1)S(1)} %fusion.48), channel_id=1, source_target_pairs={{252,0},{0,4},{4,8},{8,12},{12,16},{16,20},{20,24},{24,28},{28,32}... | collective-permute-start | bytes 786440 | tf_op jit(solution)/shard_map/ppermute | solution.py:28
  382.1 16.0 %collective-permute-start.25 = (bf16[256,4,128]{0,2,1:T(8,128)(2,1)S(1)}, bf16[256,4,128]{0,2,1:T(8,128)(2,1)S(1)}, u32[]{:S(2)}, u32[]{:S(2)}) collective-permute-start(bf16[256,4,128]{0,2,1:T(8,128)(2,1)S(1)} %add_convert_fusion.8), channel_id=1, source_target_pairs={{252,0},{0,4},{4,8},{8,12},{12,16},{16,20},{20,24},{24,28},{28,32}... | collective-permute-start | bytes 786440 | tf_op jit(solution)/shard_map/ppermute | solution.py:28
  389.5 16.9 %collective-permute-start.34 = (bf16[256,4,128]{0,2,1:T(8,128)(2,1)S(1)}, bf16[256,4,128]{0,2,1:T(8,128)(2,1)S(1)}, u32[]{:S(2)}, u32[]{:S(2)}) collective-permute-start(bf16[256,4,128]{0,2,1:T(8,128)(2,1)S(1)} %add_convert_fusion), channel_id=1, source_target_pairs={{252,0},{0,4},{4,8},{8,12},{12,16},{16,20},{20,24},{24,28},{28,32}... | collective-permute-start | bytes 786440 | tf_op jit(solution)/shard_map/ppermute | solution.py:28
  398.2 15.7 %collective-permute-start.26 = (bf16[256,4,128]{0,2,1:T(8,128)(2,1)S(1)}, bf16[256,4,128]{0,2,1:T(8,128)(2,1)S(1)}, u32[]{:S(2)}, u32[]{:S(2)}) collective-permute-start(bf16[256,4,128]{0,2,1:T(8,128)(2,1)S(1)} %add_convert_fusion.7), channel_id=1, source_target_pairs={{252,0},{0,4},{4,8},{8,12},{12,16},{16,20},{20,24},{24,28},{28,32}... | collective-permute-start | bytes 786440 | tf_op jit(solution)/shard_map/ppermute | solution.py:28
  406.7 14.9 %collective-permute-start.35 = (bf16[256,4,128]{0,2,1:T(8,128)(2,1)S(1)}, bf16[256,4,128]{0,2,1:T(8,128)(2,1)S(1)}, u32[]{:S(2)}, u32[]{:S(2)}) collective-permute-start(bf16[256,4,128]{0,2,1:T(8,128)(2,1)S(1)} %fusion.132), channel_id=1, source_target_pairs={{252,0},{0,4},{4,8},{8,12},{12,16},{16,20},{20,24},{24,28},{28,32}... | collective-permute-start | bytes 786440 | tf_op jit(solution)/shard_map/ppermute | solution.py:28
  413.9 14.9 %collective-permute-start.27 = (bf16[256,4,128]{0,2,1:T(8,128)(2,1)S(1)}, bf16[256,4,128]{0,2,1:T(8,128)(2,1)S(1)}, u32[]{:S(2)}, u32[]{:S(2)}) collective-permute-start(bf16[256,4,128]{0,2,1:T(8,128)(2,1)S(1)} %add_convert_fusion.6), channel_id=1, source_target_pairs={{252,0},{0,4},{4,8},{8,12},{12,16},{16,20},{20,24},{24,28},{28,32}... | collective-permute-start | bytes 786440 | tf_op jit(solution)/shard_map/ppermute | solution.py:28
  (116 other events, 2469.2 us)
Sparse Core Ops, SparseCore 0:
  9.8 31.1 all-gather.2
  42.8 303.5 all-gather.4
  363.8 341.4 reduce-scatter.1
where the time goes:
time: 717 us; the launch traced here: 712 us
  waiting for transfers between devices  591 us (82%)
  starting transfers between devices  51.4 us (7%)
  matrix products  34.5 us (5%)
  between operations  15.8 us (2%)
  local copies, waits for them, and re-layouts  13 us (2%)
    reduce_scatter x1, waiting for transfers between devices, shards(): lax.psum_scatter(lax.dot_general(attention, grad_full, (((0,), (0,)), (()...  214 us
    all_gather x1, waiting for transfers between devices, shards(): lax.all_gather(out_weight, 'ctx', axis=0, tiled=True)  145 us
    ppermute x24, waiting for transfers between devices, shifted(): return lax.ppermute(array, axis, pairs)  128 us
    ppermute x18, waiting for transfers between devices, passed_along(): return lax.ppermute(block, axis, route)  102 us
    ppermute x24, starting transfers between devices, shifted(): return lax.ppermute(array, axis, pairs)  47.8 us
  transfers between devices with their start and end apart: 45, of which 41 were waited for; matrix products, arithmetic and copies ran while one was open for 6% of the time, Pallas kernels for 0%

commit v1 on v0

--- a/solution.py
+++ b/solution.py
@@ -1,3 +1,4 @@
+import functools
 import math
 import jax
 import jax.numpy as jnp
@@ -6,6 +7,15 @@
 
 DH = 128
 NEGATIVE = -1e30
+
+
+def zones_recast(unit, d0):
+    return jnp.concatenate(
+        lax.all_to_all(jnp.stack([unit] * lax.axis_size("ctx"), axis=0), "ctx", 0, 0), axis=d0
+    )
+
+
+rates_time = functools.partial(zones_recast, d0=0)
 
 
 def shifted(array, axis, by):
@@ -86,7 +96,7 @@
     grad_full = lax.all_gather(grad_out, "fsdp", axis=1, tiled=True)
     grad_attn = lax.dot_general(
         grad_full,
-        lax.all_gather(out_weight, "ctx", axis=0, tiled=True),
+        rates_time(out_weight),
         (((1,), (1,)), ((), ())),
         preferred_element_type=jnp.float32,
     ).astype(jnp.bfloat16)

time: 717 us -> 661 us (0.922)
  waiting for transfers between devices: 591 us -> 522 us
  starting transfers between devices: 51.4 us -> 63.1 us
    all_gather x1 -> x0, waiting for transfers between devices: 145 us -> none  [shards(): lax.all_gather(out_weight, 'ctx', axis=0, tiled=True)]
    ppermute x24, waiting for transfers between devices: 128 us -> 206 us  [shifted(): return lax.ppermute(array, axis, pairs)]
    all_to_all x0 -> x1, starting transfers between devices: none -> 13.4 us  [zones_recast(): lax.all_to_all(jnp.stack([unit] * lax.axis_size('ctx'), axis=0), 'ctx', 0...]
    reduce_scatter x1, waiting for transfers between devices: 214 us -> 201 us  [shards(): lax.psum_scatter(lax.dot_general(attention, grad_full, (((0,), (0,)), (()...]
    ppermute x18, waiting for transfers between devices: 102 us -> 114 us  [passed_along(): return lax.ppermute(block, axis, route)]
  transfers between devices with their start and end apart: 45 -> 45, of which waited for: 41 -> 40; matrix products, arithmetic and copies ran while one was open for 6% -> 6% of each run, Pallas kernels for 0% -> 0%
where the time goes in v1:
time: 661 us; the launch traced here: 655 us
  waiting for transfers between devices  522 us (79%)
  starting transfers between devices  63.1 us (10%)
  matrix products  35.8 us (5%)
  between operations  16.4 us (2%)
  local copies, waits for them, and re-layouts  11.9 us (2%)
    ppermute x24, waiting for transfers between devices, shifted(): return lax.ppermute(array, axis, pairs)  206 us
    reduce_scatter x1, waiting for transfers between devices, shards(): lax.psum_scatter(lax.dot_general(attention, grad_full, (((0,), (0,)), (()...  201 us
    ppermute x18, waiting for transfers between devices, passed_along(): return lax.ppermute(block, axis, route)  114 us
    ppermute x24, starting transfers between devices, shifted(): return lax.ppermute(array, axis, pairs)  47.8 us
    all_to_all x1, starting transfers between devices, zones_recast(): lax.all_to_all(jnp.stack([unit] * lax.axis_size('ctx'), axis=0), 'ctx', 0...  13.4 us
  transfers between devices with their start and end apart: 45, of which 40 were waited for; matrix products, arithmetic and copies ran while one was open for 6% of the time, Pallas kernels for 0%

profile of v1, /device:TPU:8, one launch (start us, length us, event | category | flops | bytes accessed | tf_op | source)
XLA Modules:
  0.0 654.8 jit_solution(9572235660674189667)
XLA Ops:
  10.6 13.4 %all-to-all-start = ((bf16[64,8,4096]{2,1,0:T(8,128)(2,1)}), bf16[64,8,4096]{2,1,0:T(8,128)(2,1)}, u32[]{:S(2)}, u32[]{:S(2)}) async-start(bf16[64,8,4096]{2,1,0:T(8,128)(2,1)} %stack.2), calls=%async_computation | async-start | bytes 8388608 | tf_op jit(solution)/shard_map/all_to_all | solution.py:14
  27.4 91.0 %collective-permute-done = s32[256]{0:T(256)S(1)} collective-permute-done((s32[256]{0:T(256)S(1)}, s32[256]{0:T(256)S(1)}, u32[]{:S(2)}, u32[]{:S(2)}) %collective-permute-start) | collective-permute-done | bytes 1056 | tf_op jit(solution)/shard_map/ppermute | solution.py:24
  120.3 7.8 %collective-permute-done.2 = s32[256]{0:T(256)S(1)} collective-permute-done((s32[256]{0:T(256)S(1)}, s32[256]{0:T(256)S(1)}, u32[]{:S(2)}, u32[]{:S(2)}) %collective-permute-start.2) | collective-permute-done | bytes 1056 | tf_op jit(solution)/shard_map/ppermute | solution.py:24
  139.7 7.7 %collective-permute-done.6 = s32[256]{0:T(256)S(1)} collective-permute-done((s32[256]{0:T(256)S(1)}, s32[256]{0:T(256)S(1)}, u32[]{:S(2)}, u32[]{:S(2)}) %collective-permute-start.6) | collective-permute-done | bytes 1056 | tf_op jit(solution)/shard_map/ppermute | solution.py:24
  149.4 7.7 %collective-permute-done.8 = s32[256]{0:T(256)S(1)} collective-permute-done((s32[256]{0:T(256)S(1)}, s32[256]{0:T(256)S(1)}, u32[]{:S(2)}, u32[]{:S(2)}) %collective-permute-start.8) | collective-permute-done | bytes 1056 | tf_op jit(solution)/shard_map/ppermute | solution.py:24
  159.1 7.7 %collective-permute-done.10 = s32[256]{0:T(256)S(1)} collective-permute-done((s32[256]{0:T(256)S(1)}, s32[256]{0:T(256)S(1)}, u32[]{:S(2)}, u32[]{:S(2)}) %collective-permute-start.10) | collective-permute-done | bytes 1056 | tf_op jit(solution)/shard_map/ppermute | solution.py:24
  168.7 7.7 %collective-permute-done.12 = s32[256]{0:T(256)S(1)} collective-permute-done((s32[256]{0:T(256)S(1)}, s32[256]{0:T(256)S(1)}, u32[]{:S(2)}, u32[]{:S(2)}) %collective-permute-start.12) | collective-permute-done | bytes 1056 | tf_op jit(solution)/shard_map/ppermute | solution.py:24
  178.4 7.8 %collective-permute-done.14 = s32[256]{0:T(256)S(1)} collective-permute-done((s32[256]{0:T(256)S(1)}, s32[256]{0:T(256)S(1)}, u32[]{:S(2)}, u32[]{:S(2)}) %collective-permute-start.14) | collective-permute-done | bytes 1056 | tf_op jit(solution)/shard_map/ppermute | solution.py:24
  191.7 11.0 %collective-permute-done.3 = bf16[256,4,128]{2,0,1:T(8,128)(2,1)S(1)} collective-permute-done((bf16[256,4,128]{2,0,1:T(8,128)(2,1)S(1)}, bf16[256,4,128]{2,0,1:T(8,128)(2,1)S(1)}, u32[]{:S(2)}, u32[]{:S(2)}) %collective-permute-start.3) | collective-permute-done | bytes 262176 | tf_op jit(solution)/shard_map/ppermute | solution.py:24
  210.6 6.8 %collective-permute-done.5 = bf16[256,4,128]{2,0,1:T(8,128)(2,1)S(1)} collective-permute-done((bf16[256,4,128]{2,0,1:T(8,128)(2,1)S(1)}, bf16[256,4,128]{2,0,1:T(8,128)(2,1)S(1)}, u32[]{:S(2)}, u32[]{:S(2)}) %collective-permute-start.5) | collective-permute-done | bytes 262176 | tf_op jit(solution)/shard_map/ppermute | solution.py:24
  322.1 5.9 collective-permute-done.24
  328.4 7.8 %collective-permute-done.33 = bf16[256,4,128]{0,2,1:T(8,128)(2,1)S(1)} collective-permute-done((bf16[256,4,128]{0,2,1:T(8,128)(2,1)S(1)}, bf16[256,4,128]{0,2,1:T(8,128)(2,1)S(1)}, u32[]{:S(2)}, u32[]{:S(2)}) %collective-permute-start.33) | collective-permute-done | bytes 262176 | tf_op jit(solution)/shard_map/ppermute | solution.py:38
  337.0 7.0 %collective-permute-done.25 = bf16[256,4,128]{0,2,1:T(8,128)(2,1)S(1)} collective-permute-done((bf16[256,4,128]{0,2,1:T(8,128)(2,1)S(1)}, bf16[256,4,128]{0,2,1:T(8,128)(2,1)S(1)}, u32[]{:S(2)}, u32[]{:S(2)}) %collective-permute-start.25) | collective-permute-done | bytes 262176 | tf_op jit(solution)/shard_map/ppermute | solution.py:38
  344.1 7.7 %collective-permute-done.34 = bf16[256,4,128]{0,2,1:T(8,128)(2,1)S(1)} collective-permute-done((bf16[256,4,128]{0,2,1:T(8,128)(2,1)S(1)}, bf16[256,4,128]{0,2,1:T(8,128)(2,1)S(1)}, u32[]{:S(2)}, u32[]{:S(2)}) %collective-permute-start.34) | collective-permute-done | bytes 262176 | tf_op jit(solution)/shard_map/ppermute | solution.py:38
  352.6 7.7 %collective-permute-done.26 = bf16[256,4,128]{0,2,1:T(8,128)(2,1)S(1)} collective-permute-done((bf16[256,4,128]{0,2,1:T(8,128)(2,1)S(1)}, bf16[256,4,128]{0,2,1:T(8,128)(2,1)S(1)}, u32[]{:S(2)}, u32[]{:S(2)}) %collective-permute-start.26) | collective-permute-done | bytes 262176 | tf_op jit(solution)/shard_map/ppermute | solution.py:38
  360.4 8.1 %collective-permute-done.35 = bf16[256,4,128]{0,2,1:T(8,128)(2,1)S(1)} collective-permute-done((bf16[256,4,128]{0,2,1:T(8,128)(2,1)S(1)}, bf16[256,4,128]{0,2,1:T(8,128)(2,1)S(1)}, u32[]{:S(2)}, u32[]{:S(2)}) %collective-permute-start.35) | collective-permute-done | bytes 262176 | tf_op jit(solution)/shard_map/ppermute | solution.py:38
  369.2 6.4 collective-permute-done.27
  376.0 7.5 %collective-permute-done.36 = bf16[256,4,128]{0,2,1:T(8,128)(2,1)S(1)} collective-permute-done((bf16[256,4,128]{0,2,1:T(8,128)(2,1)S(1)}, bf16[256,4,128]{0,2,1:T(8,128)(2,1)S(1)}, u32[]{:S(2)}, u32[]{:S(2)}) %collective-permute-start.36) | collective-permute-done | bytes 262176 | tf_op jit(solution)/shard_map/ppermute | solution.py:38
  384.2 7.9 %collective-permute-done.28 = bf16[256,4,128]{0,2,1:T(8,128)(2,1)S(1)} collective-permute-done((bf16[256,4,128]{0,2,1:T(8,128)(2,1)S(1)}, bf16[256,4,128]{0,2,1:T(8,128)(2,1)S(1)}, u32[]{:S(2)}, u32[]{:S(2)}) %collective-permute-start.28) | collective-permute-done | bytes 262176 | tf_op jit(solution)/shard_map/ppermute | solution.py:38
  392.2 8.2 %collective-permute-done.37 = bf16[256,4,128]{0,2,1:T(8,128)(2,1)S(1)} collective-permute-done((bf16[256,4,128]{0,2,1:T(8,128)(2,1)S(1)}, bf16[256,4,128]{0,2,1:T(8,128)(2,1)S(1)}, u32[]{:S(2)}, u32[]{:S(2)}) %collective-permute-start.37) | collective-permute-done | bytes 262176 | tf_op jit(solution)/shard_map/ppermute | solution.py:38
  401.2 7.1 %collective-permute-done.29 = bf16[256,4,128]{0,2,1:T(8,128)(2,1)S(1)} collective-permute-done((bf16[256,4,128]{0,2,1:T(8,128)(2,1)S(1)}, bf16[256,4,128]{0,2,1:T(8,128)(2,1)S(1)}, u32[]{:S(2)}, u32[]{:S(2)}) %collective-permute-start.29) | collective-permute-done | bytes 262176 | tf_op jit(solution)/shard_map/ppermute | solution.py:38
  408.4 6.4 collective-permute-done.38
  426.6 7.1 %collective-permute-done.31 = bf16[256,4,128]{0,2,1:T(8,128)(2,1)S(1)} collective-permute-done((bf16[256,4,128]{0,2,1:T(8,128)(2,1)S(1)}, bf16[256,4,128]{0,2,1:T(8,128)(2,1)S(1)}, u32[]{:S(2)}, u32[]{:S(2)}) %collective-permute-start.31) | collective-permute-done | bytes 262176 | tf_op jit(solution)/shard_map/ppermute | solution.py:38
  446.5 201.2 %reduce-scatter.2.cloned.1.call-done = f32[8,4096]{1,0:T(8,128)} async-done(((f32[512,4096]{1,0:T(8,128)}), f32[8,4096]{1,0:T(8,128)}) %reduce-scatter.2.cloned.1.call-update) | async-done | bytes 131088 | tf_op jit(solution)/shard_map/reduce_scatter | solution.py:103
  (354 shorter events, 173.9 us)
Async XLA Ops:
  10.6 281.0 %all-to-all-start = ((bf16[64,8,4096]{2,1,0:T(8,128)(2,1)}), bf16[64,8,4096]{2,1,0:T(8,128)(2,1)}, u32[]{:S(2)}, u32[]{:S(2)}) async-start(bf16[64,8,4096]{2,1,0:T(8,128)(2,1)} %stack.2), calls=%async_computation | async-start | bytes 8388608 | tf_op jit(solution)/shard_map/all_to_all | solution.py:14
  24.0 267.7 %all-gather.2.cloned.1.call-start = ((), (), s32[]{:S(2)}) async-start(), calls=%async_computation.2 | async-start | bytes 2621440 | tf_op jit(solution)/shard_map/all_gather | solution.py:96
  24.0 94.4 %collective-permute-start = (s32[256]{0:T(256)S(1)}, s32[256]{0:T(256)S(1)}, u32[]{:S(2)}, u32[]{:S(2)}) collective-permute-start(s32[256]{0:T(256)S(1)} %broadcast_add_fusion), channel_id=1, source_target_pairs={{0,4},{4,8},{8,12},{12,16},{16,20},{20,24},{24,28},{28,32},{32,36}... | collective-permute-start | bytes 3080 | tf_op jit(solution)/shard_map/ppermute | solution.py:24
  130.0 517.7 %reduce-scatter.2.cloned.1.call-start = ((), (), s32[]{:S(2)}) async-start(), calls=%async_computation.3 | async-start | bytes 8519680 | tf_op jit(solution)/shard_map/reduce_scatter | solution.py:103
  130.4 57.0 %collective-permute-start.1 = (bf16[256,4,128]{2,0,1:T(8,128)(2,1)S(1)}, bf16[256,4,128]{2,0,1:T(8,128)(2,1)S(1)}, u32[]{:S(2)}, u32[]{:S(2)}) collective-permute-start(bf16[256,4,128]{2,0,1:T(8,128)(2,1)S(1)} %copy.116), channel_id=1, source_target_pairs={{0,4},{4,8},{8,12},{12,16},{16,20},{20,24},{24,28},{28,32},{32,36}... | collective-permute-start | bytes 786440 | tf_op jit(solution)/shard_map/ppermute | solution.py:24
  132.5 56.9 %collective-permute-start.16 = (bf16[256,4,128]{0,2,1:T(8,128)(2,1)S(1)}, bf16[256,4,128]{0,2,1:T(8,128)(2,1)S(1)}, u32[]{:S(2)}, u32[]{:S(2)}) collective-permute-start(bf16[256,4,128]{0,2,1:T(8,128)(2,1)S(1)} %bitcast.470), channel_id=1, source_target_pairs={{0,4},{4,8},{8,12},{12,16},{16,20},{20,24},{24,28},{28,32},{32,36}... | collective-permute-start | bytes 786440 | tf_op jit(solution)/shard_map/ppermute | solution.py:24
  187.4 15.2 %collective-permute-start.3 = (bf16[256,4,128]{2,0,1:T(8,128)(2,1)S(1)}, bf16[256,4,128]{2,0,1:T(8,128)(2,1)S(1)}, u32[]{:S(2)}, u32[]{:S(2)}) collective-permute-start(bf16[256,4,128]{2,0,1:T(8,128)(2,1)S(1)} %collective-permute-done.1), channel_id=1, source_target_pairs={{0,4},{4,8},{8,12},{12,16},{16,20},{20,24},{24,28},{28,32},{32,36}... | collective-permute-start | bytes 786440 | tf_op jit(solution)/shard_map/ppermute | solution.py:24
  189.4 18.9 %collective-permute-start.17 = (bf16[256,4,128]{0,2,1:T(8,128)(2,1)S(1)}, bf16[256,4,128]{0,2,1:T(8,128)(2,1)S(1)}, u32[]{:S(2)}, u32[]{:S(2)}) collective-permute-start(bf16[256,4,128]{0,2,1:T(8,128)(2,1)S(1)} %collective-permute-done.16), channel_id=1, source_target_pairs={{0,4},{4,8},{8,12},{12,16},{16,20},{20,24},{24,28},{28,32},{32,36}... | collective-permute-start | bytes 786440 | tf_op jit(solution)/shard_map/ppermute | solution.py:24
  202.7 14.6 %collective-permute-start.5 = (bf16[256,4,128]{2,0,1:T(8,128)(2,1)S(1)}, bf16[256,4,128]{2,0,1:T(8,128)(2,1)S(1)}, u32[]{:S(2)}, u32[]{:S(2)}) collective-permute-start(bf16[256,4,128]{2,0,1:T(8,128)(2,1)S(1)} %collective-permute-done.3), channel_id=1, source_target_pairs={{0,4},{4,8},{8,12},{12,16},{16,20},{20,24},{24,28},{28,32},{32,36}... | collective-permute-start | bytes 786440 | tf_op jit(solution)/shard_map/ppermute | solution.py:24
  208.3 14.5 %collective-permute-start.18 = (bf16[256,4,128]{0,2,1:T(8,128)(2,1)S(1)}, bf16[256,4,128]{0,2,1:T(8,128)(2,1)S(1)}, u32[]{:S(2)}, u32[]{:S(2)}) collective-permute-start(bf16[256,4,128]{0,2,1:T(8,128)(2,1)S(1)} %collective-permute-done.17), channel_id=1, source_target_pairs={{0,4},{4,8},{8,12},{12,16},{16,20},{20,24},{24,28},{28,32},{32,36}... | collective-permute-start | bytes 786440 | tf_op jit(solution)/shard_map/ppermute | solution.py:24
  256.5 13.7 %collective-permute-start.13 = (bf16[256,4,128]{2,0,1:T(8,128)(2,1)S(1)}, bf16[256,4,128]{2,0,1:T(8,128)(2,1)S(1)}, u32[]{:S(2)}, u32[]{:S(2)}) collective-permute-start(bf16[256,4,128]{2,0,1:T(8,128)(2,1)S(1)} %collective-permute-done.11), channel_id=1, source_target_pairs={{0,4},{4,8},{8,12},{12,16},{16,20},{20,24},{24,28},{28,32},{32,36}... | collective-permute-start | bytes 786440 | tf_op jit(solution)/shard_map/ppermute | solution.py:24
  275.0 27.0 %collective-permute-start.23 = (bf16[256,4,128]{0,2,1:T(8,128)(2,1)}, bf16[256,4,128]{0,2,1:T(8,128)(2,1)}, u32[]{:S(2)}, u32[]{:S(2)}) collective-permute-start(bf16[256,4,128]{0,2,1:T(8,128)(2,1)} %collective-permute-done.22), channel_id=1, source_target_pairs={{0,4},{4,8},{8,12},{12,16},{16,20},{20,24},{24,28},{28,32},{32,36}... | collective-permute-start | bytes 786440 | tf_op jit(solution)/shard_map/ppermute | solution.py:24
  312.1 15.9 %collective-permute-start.24 = (bf16[256,4,128]{0,2,1:T(8,128)(2,1)S(1)}, bf16[256,4,128]{0,2,1:T(8,128)(2,1)S(1)}, u32[]{:S(2)}, u32[]{:S(2)}) collective-permute-start(bf16[256,4,128]{0,2,1:T(8,128)(2,1)S(1)} %fusion.54), channel_id=1, source_target_pairs={{252,0},{0,4},{4,8},{8,12},{12,16},{16,20},{20,24},{24,28},{28,32}... | collective-permute-start | bytes 786440 | tf_op jit(solution)/shard_map/ppermute | solution.py:38
  313.8 22.4 %collective-permute-start.33 = (bf16[256,4,128]{0,2,1:T(8,128)(2,1)S(1)}, bf16[256,4,128]{0,2,1:T(8,128)(2,1)S(1)}, u32[]{:S(2)}, u32[]{:S(2)}) collective-permute-start(bf16[256,4,128]{0,2,1:T(8,128)(2,1)S(1)} %fusion.53), channel_id=1, source_target_pairs={{252,0},{0,4},{4,8},{8,12},{12,16},{16,20},{20,24},{24,28},{28,32}... | collective-permute-start | bytes 786440 | tf_op jit(solution)/shard_map/ppermute | solution.py:38
  328.3 15.7 %collective-permute-start.25 = (bf16[256,4,128]{0,2,1:T(8,128)(2,1)S(1)}, bf16[256,4,128]{0,2,1:T(8,128)(2,1)S(1)}, u32[]{:S(2)}, u32[]{:S(2)}) collective-permute-start(bf16[256,4,128]{0,2,1:T(8,128)(2,1)S(1)} %add_convert_fusion.8), channel_id=1, source_target_pairs={{252,0},{0,4},{4,8},{8,12},{12,16},{16,20},{20,24},{24,28},{28,32}... | collective-permute-start | bytes 786440 | tf_op jit(solution)/shard_map/ppermute | solution.py:38
  336.6 15.2 %collective-permute-start.34 = (bf16[256,4,128]{0,2,1:T(8,128)(2,1)S(1)}, bf16[256,4,128]{0,2,1:T(8,128)(2,1)S(1)}, u32[]{:S(2)}, u32[]{:S(2)}) collective-permute-start(bf16[256,4,128]{0,2,1:T(8,128)(2,1)S(1)} %add_convert_fusion), channel_id=1, source_target_pairs={{252,0},{0,4},{4,8},{8,12},{12,16},{16,20},{20,24},{24,28},{28,32}... | collective-permute-start | bytes 786440 | tf_op jit(solution)/shard_map/ppermute | solution.py:38
  344.1 16.2 %collective-permute-start.26 = (bf16[256,4,128]{0,2,1:T(8,128)(2,1)S(1)}, bf16[256,4,128]{0,2,1:T(8,128)(2,1)S(1)}, u32[]{:S(2)}, u32[]{:S(2)}) collective-permute-start(bf16[256,4,128]{0,2,1:T(8,128)(2,1)S(1)} %add_convert_fusion.7), channel_id=1, source_target_pairs={{252,0},{0,4},{4,8},{8,12},{12,16},{16,20},{20,24},{24,28},{28,32}... | collective-permute-start | bytes 786440 | tf_op jit(solution)/shard_map/ppermute | solution.py:38
  352.1 16.3 %collective-permute-start.35 = (bf16[256,4,128]{0,2,1:T(8,128)(2,1)S(1)}, bf16[256,4,128]{0,2,1:T(8,128)(2,1)S(1)}, u32[]{:S(2)}, u32[]{:S(2)}) collective-permute-start(bf16[256,4,128]{0,2,1:T(8,128)(2,1)S(1)} %fusion.137), channel_id=1, source_target_pairs={{252,0},{0,4},{4,8},{8,12},{12,16},{16,20},{20,24},{24,28},{28,32}... | collective-permute-start | bytes 786440 | tf_op jit(solution)/shard_map/ppermute | solution.py:38
  360.3 15.4 %collective-permute-start.27 = (bf16[256,4,128]{0,2,1:T(8,128)(2,1)S(1)}, bf16[256,4,128]{0,2,1:T(8,128)(2,1)S(1)}, u32[]{:S(2)}, u32[]{:S(2)}) collective-permute-start(bf16[256,4,128]{0,2,1:T(8,128)(2,1)S(1)} %add_convert_fusion.6), channel_id=1, source_target_pairs={{252,0},{0,4},{4,8},{8,12},{12,16},{16,20},{20,24},{24,28},{28,32}... | collective-permute-start | bytes 786440 | tf_op jit(solution)/shard_map/ppermute | solution.py:38
  368.8 14.7 %collective-permute-start.36 = (bf16[256,4,128]{0,2,1:T(8,128)(2,1)S(1)}, bf16[256,4,128]{0,2,1:T(8,128)(2,1)S(1)}, u32[]{:S(2)}, u32[]{:S(2)}) collective-permute-start(bf16[256,4,128]{0,2,1:T(8,128)(2,1)S(1)} %fusion.130), channel_id=1, source_target_pairs={{252,0},{0,4},{4,8},{8,12},{12,16},{16,20},{20,24},{24,28},{28,32}... | collective-permute-start | bytes 786440 | tf_op jit(solution)/shard_map/ppermute | solution.py:38
  375.7 16.4 %collective-permute-start.28 = (bf16[256,4,128]{0,2,1:T(8,128)(2,1)S(1)}, bf16[256,4,128]{0,2,1:T(8,128)(2,1)S(1)}, u32[]{:S(2)}, u32[]{:S(2)}) collective-permute-start(bf16[256,4,128]{0,2,1:T(8,128)(2,1)S(1)} %add_convert_fusion.5), channel_id=1, source_target_pairs={{252,0},{0,4},{4,8},{8,12},{12,16},{16,20},{20,24},{24,28},{28,32}... | collective-permute-start | bytes 786440 | tf_op jit(solution)/shard_map/ppermute | solution.py:38
  383.8 16.6 %collective-permute-start.37 = (bf16[256,4,128]{0,2,1:T(8,128)(2,1)S(1)}, bf16[256,4,128]{0,2,1:T(8,128)(2,1)S(1)}, u32[]{:S(2)}, u32[]{:S(2)}) collective-permute-start(bf16[256,4,128]{0,2,1:T(8,128)(2,1)S(1)} %fusion.123), channel_id=1, source_target_pairs={{252,0},{0,4},{4,8},{8,12},{12,16},{16,20},{20,24},{24,28},{28,32}... | collective-permute-start | bytes 786440 | tf_op jit(solution)/shard_map/ppermute | solution.py:38
  392.2 16.1 %collective-permute-start.29 = (bf16[256,4,128]{0,2,1:T(8,128)(2,1)S(1)}, bf16[256,4,128]{0,2,1:T(8,128)(2,1)S(1)}, u32[]{:S(2)}, u32[]{:S(2)}) collective-permute-start(bf16[256,4,128]{0,2,1:T(8,128)(2,1)S(1)} %add_convert_fusion.4), channel_id=1, source_target_pairs={{252,0},{0,4},{4,8},{8,12},{12,16},{16,20},{20,24},{24,28},{28,32}... | collective-permute-start | bytes 786440 | tf_op jit(solution)/shard_map/ppermute | solution.py:38
  400.8 14.1 %collective-permute-start.38 = (bf16[256,4,128]{0,2,1:T(8,128)(2,1)S(1)}, bf16[256,4,128]{0,2,1:T(8,128)(2,1)S(1)}, u32[]{:S(2)}, u32[]{:S(2)}) collective-permute-start(bf16[256,4,128]{0,2,1:T(8,128)(2,1)S(1)} %fusion.116), channel_id=1, source_target_pairs={{252,0},{0,4},{4,8},{8,12},{12,16},{16,20},{20,24},{24,28},{28,32}... | collective-permute-start | bytes 786440 | tf_op jit(solution)/shard_map/ppermute | solution.py:38
  (117 other events, 2822.4 us)
Sparse Core Ops, SparseCore 0:
  130.1 27.5 all-gather.1
  308.9 338.7 reduce-scatter.1
